TPU v7x, 256 devices: a whole 4x4x8 slice. The times are simulated.
256 devices in a mesh: ctx: 32 (over x, z_lo, y), head: 8 (over z_hi, core).
Axes of the slice: x: 4, y: 4, z: 8 (z_hi: 4, z_lo: 2; z = z_hi * 2 + z_lo), core: 2. Of those that a mesh axis runs over, the one named last changes fastest.
Arguments:
- tokens: bfloat16 [8192, 4096], P('ctx', 'head'), may hold values from -6 to 6
- cotangent: bfloat16 [8192, 4096], P('ctx', 'head'), may hold values from -0.1796875 to 0.1796875
- expert_ids: int32 [8192, 2], P('ctx'), may hold values from 0 to 31, all different within a row; in each aligned block of 256 rows (0 to 255, 256 to 511, ...) at most 24 rows name the same one
- w_router: bfloat16 [4096, 32], P('head'), may hold values from -0.09375 to 0.09375
- w_gate: bfloat16 [32, 1408, 4096], P('ctx', None, 'head'), may hold values from -0.09375 to 0.09375
- w_up: bfloat16 [32, 1408, 4096], P('ctx', None, 'head'), may hold values from -0.09375 to 0.09375
- w_down: bfloat16 [32, 1408, 4096], P('ctx', None, 'head'), may hold values from -0.15625 to 0.15625
Outputs:
- mixed: bfloat16 [8192, 4096], P('ctx', 'head')
- grad_tokens: bfloat16 [8192, 4096], P('ctx', 'head')
- grad_router: float32 [4096, 32], P('head')
- grad_gate: bfloat16 [32, 1408, 4096], P('ctx', None, 'head')
- grad_up: bfloat16 [32, 1408, 4096], P('ctx', None, 'head')
- grad_down: bfloat16 [32, 1408, 4096], P('ctx', None, 'head')
Inputs may be any that keep to these rules, and one draw needn't show every extreme that they name: `expert_ids`: each row names 2 different experts. Within the rows of one device (aligned blocks of 256 rows) no expert is named by more than 24 rows, a bound that some block reaches.
All inputs are finite; a program needn't handle non-finite values.
Results may differ from a plain program's by a relative error of at most 0.023.
Values may be sent and summed in bfloat16 or wider, within the bound.
No kernel may reach another device: no remote copies, remote signals or barrier semaphores. Data moves between devices by JAX's collectives and lax.ppermute only.
A program may use at most 64 MiB of HBM per device.

v0:
```python
import jax
import jax.numpy as jnp
from jax import lax
from jax.sharding import PartitionSpec as P


def contract_rows(left, right):
    return lax.dot_general(
        left, right, (((0,), (0,)), ((), ())), preferred_element_type=jnp.float32
    )


def contract_last(left, right):
    return lax.dot_general(
        left, right, (((1,), (1,)), ((), ())), preferred_element_type=jnp.float32
    )


def activations(gate_pre, up_pre, back_proj, prob_rows):
    sigma = jax.nn.sigmoid(gate_pre)
    active = gate_pre * sigma
    hidden = (active * up_pre).astype(jnp.bfloat16)
    hidden_grad = prob_rows[:, None] * back_proj
    gate_grad = (hidden_grad * up_pre * sigma * (1.0 + gate_pre * (1.0 - sigma))).astype(
        jnp.bfloat16
    )
    up_grad = (hidden_grad * active).astype(jnp.bfloat16)
    return (hidden, gate_grad, up_grad)


def local(tokens, cotangent, expert_ids, w_router, w_gate, w_up, w_down):
    ctx_count = lax.axis_size("ctx")
    tok_rows = tokens.shape[0]
    shard_width = tokens.shape[1]
    pick_count = expert_ids.shape[1]
    experts = w_router.shape[1]
    capacity = 3 * tok_rows * pick_count // (2 * experts)
    partial_logits = jnp.dot(tokens, w_router, preferred_element_type=jnp.float32)
    onehot = (expert_ids[:, :, None] == jnp.arange(experts, dtype=jnp.int32)[None, None, :]).astype(
        jnp.float32
    )
    chosen = lax.psum(jnp.sum(partial_logits[:, None, :] * onehot, axis=2), "head")
    prob_pairs = jnp.stack(
        [jax.nn.sigmoid(chosen[:, 0] - chosen[:, 1]), jax.nn.sigmoid(chosen[:, 1] - chosen[:, 0])],
        axis=1,
    )
    flat_ids = expert_ids.reshape(-1)
    id_hits = (flat_ids[:, None] == jnp.arange(experts, dtype=jnp.int32)[None, :]).astype(jnp.int32)
    places = jnp.sum((jnp.cumsum(id_hits, axis=0) - 1) * id_hits, axis=1)
    slot_index = flat_ids * capacity + places
    slot_table = (
        jnp.zeros((experts * capacity,), jnp.int32)
        .at[slot_index]
        .set(jnp.arange(tok_rows * pick_count, dtype=jnp.int32) + 1)
    )
    occupied = slot_table > 0
    source = jnp.maximum(slot_table - 1, 0)
    row_index = source // pick_count
    prob_send = jnp.where(occupied, prob_pairs.reshape(-1)[source], jnp.float32(0.0)).reshape(
        experts, capacity
    )

    def pack_rows(values):
        picked = jnp.where(occupied[:, None], values[row_index], jnp.zeros((), values.dtype))
        return picked.reshape(experts, capacity, values.shape[1])

    recv_x, recv_g, recv_p = (
        lax.all_to_all(pack_rows(tokens), "ctx", split_axis=0, concat_axis=0, tiled=True),
        lax.all_to_all(pack_rows(cotangent), "ctx", split_axis=0, concat_axis=0, tiled=True),
        lax.all_to_all(
            prob_send.astype(jnp.bfloat16), "ctx", split_axis=0, concat_axis=0, tiled=True
        ).astype(prob_send.dtype),
    )
    slot_count = recv_x.shape[0] * recv_x.shape[1]
    x_rows = recv_x.reshape(slot_count, shard_width)
    cot_rows = recv_g.reshape(slot_count, shard_width)
    prob_rows = recv_p.reshape(slot_count)
    gate_w = w_gate[0]
    up_w = w_up[0]
    down_w = w_down[0]
    gate_part = contract_last(x_rows, gate_w)
    up_part = contract_last(x_rows, up_w)
    back_part = contract_last(cot_rows, down_w)
    gate_pre, up_pre, back_proj = (
        lax.psum(gate_part.astype(jnp.bfloat16), "head").astype(jnp.float32),
        lax.psum(up_part.astype(jnp.bfloat16), "head").astype(jnp.float32),
        lax.psum(back_part.astype(jnp.bfloat16), "head").astype(jnp.float32),
    )
    hidden, gate_grad, up_grad = activations(gate_pre, up_pre, back_proj, prob_rows)
    out_rows = jnp.dot(hidden, down_w, preferred_element_type=jnp.float32).astype(jnp.bfloat16)
    dx_rows = (
        jnp.dot(gate_grad, gate_w, preferred_element_type=jnp.float32)
        + jnp.dot(up_grad, up_w, preferred_element_type=jnp.float32)
    ).astype(jnp.bfloat16)
    hidden_kept = lax.optimization_barrier(hidden)
    scaled = (prob_rows[:, None] * hidden_kept.astype(jnp.float32)).astype(jnp.bfloat16)
    grad_down = contract_rows(scaled, cot_rows).astype(jnp.bfloat16)[None]
    grad_gate = contract_rows(gate_grad, x_rows).astype(jnp.bfloat16)[None]
    grad_up = contract_rows(up_grad, x_rows).astype(jnp.bfloat16)[None]
    back_out, back_dx = (
        lax.all_to_all(
            out_rows.reshape(ctx_count, capacity, shard_width),
            "ctx",
            split_axis=0,
            concat_axis=0,
            tiled=True,
        ),
        lax.all_to_all(
            dx_rows.reshape(ctx_count, capacity, shard_width),
            "ctx",
            split_axis=0,
            concat_axis=0,
            tiled=True,
        ),
    )
    out_pairs = back_out.reshape(experts * capacity, shard_width)[slot_index].reshape(
        tok_rows, pick_count, shard_width
    )
    dx_pairs = back_dx.reshape(experts * capacity, shard_width)[slot_index].reshape(
        tok_rows, pick_count, shard_width
    )
    mixed = jnp.sum(prob_pairs[:, :, None] * out_pairs.astype(jnp.float32), axis=1).astype(
        jnp.bfloat16
    )
    score_part = jnp.sum(
        cotangent.astype(jnp.float32)[:, None, :] * out_pairs.astype(jnp.float32), axis=2
    )
    score_grad = lax.psum(score_part, "head")
    logit_lead = prob_pairs[:, 0] * prob_pairs[:, 1] * (score_grad[:, 0] - score_grad[:, 1])
    logit_grad = jnp.stack([logit_lead, -logit_lead], axis=1)
    dense_grad = jnp.sum(logit_grad[:, :, None] * onehot, axis=1)
    router_term = jnp.dot(
        dense_grad, w_router.astype(jnp.float32).T, precision=lax.Precision.HIGHEST
    )
    grad_tokens = (
        dx_pairs[:, 0].astype(jnp.float32) + dx_pairs[:, 1].astype(jnp.float32) + router_term
    ).astype(jnp.bfloat16)
    router_part = jnp.dot(tokens.astype(jnp.float32).T, dense_grad, precision=lax.Precision.HIGHEST)
    grad_router = lax.psum(router_part, "ctx")
    return (mixed, grad_tokens, grad_router, grad_gate, grad_up, grad_down)


def solution(mesh):
    placed = (
        P("ctx", "head"),
        P("ctx", "head"),
        P("ctx", None),
        P("head", None),
        P("ctx", None, "head"),
        P("ctx", None, "head"),
        P("ctx", None, "head"),
    )
    return jax.shard_map(
        local,
        mesh=mesh,
        in_specs=placed,
        out_specs=(
            P("ctx", "head"),
            P("ctx", "head"),
            P("head", None),
            P("ctx", None, "head"),
            P("ctx", None, "head"),
            P("ctx", None, "head"),
        ),
        check_vma=False,
    )
```

profile of v0, /device:TPU:64, one launch (start us, length us, event | category | flops | bytes accessed | tf_op | source)
XLA Modules:
  0.0 605.1 jit_solution(14181950294091375107)
XLA Ops:
  15.3 15.2 %psum.42 = f32[256,2]{0,1:T(2,128)S(1)} all-reduce(f32[256,2]{0,1:T(2,128)S(1)} %select_reduce_fusion.1), channel_id=1, replica_groups=mesh['ctx'=32,'head'=8] {'head'}, use_global_device_ids=true, to_apply=%region_1.0 | all-reduce | flops 512 | bytes 4096 | tf_op jit(solution)/shard_map/psum | solution.py:42
  30.9 5.0 gather_fusion.2
  36.6 2.7 gather_fusion
  39.3 2.7 gather_fusion.3
  43.1 20.9 %all_to_all.26 = bf16[32,24,512]{2,1,0:T(8,128)(2,1)S(1)} all-to-all(bf16[32,24,512]{2,1,0:T(8,128)(2,1)S(1)} %get-tuple-element.21), channel_id=1, replica_groups=mesh['ctx'=32,'head'=8] {'ctx'}, dimensions={0} | all-to-all | bytes 1572864 | tf_op jit(solution)/shard_map/all_to_all | solution.py:68
  64.0 4.4 all-to-all-start.3
  68.4 2.8 convolution_convert_fusion.1
  71.2 2.8 convolution_convert_fusion.2
  74.0 6.5 %all-to-all-done.3 = bf16[32,24,512]{2,1,0:T(8,128)(2,1)S(1)} async-done(((bf16[32,24,512]{2,1,0:T(8,128)(2,1)}), bf16[32,24,512]{2,1,0:T(8,128)(2,1)S(1)}, u32[]{:S(2)}, u32[]{:S(2)}) %all-to-all-start.3) | async-done | bytes 786464 | tf_op jit(solution)/shard_map/all_to_all | solution.py:69
  80.6 4.4 convolution_convert_fusion
  85.8 12.5 %all_to_all.27 = bf16[32,1,24]{2,1,0:T(2,128)(2,1)S(1)} all-to-all(bf16[32,1,24]{2,1,0:T(2,128)(2,1)S(1)} %convert_element_type.137), channel_id=1, replica_groups=mesh['ctx'=32,'head'=8] {'ctx'}, dimensions={0} | all-to-all | bytes 3072 | tf_op jit(solution)/shard_map/all_to_all | solution.py:70
  98.4 137.6 %all-reduce.6.cloned.1.call-done = (bf16[768,1408]{1,0:T(8,128)(2,1)}, bf16[768,1408]{1,0:T(8,128)(2,1)}, bf16[768,1408]{1,0:T(8,128)(2,1)}) async-done(((bf16[768,1408]{1,0:T(8,128)(2,1)}, bf16[768,1408]{1,0:T(8,128)(2,1)}, bf16[768,1408]{1,0:T(8,128)(2,1)}), (bf16[768,1408]{1,0:T(8,128)(2,1)}, bf16[768,1408]{1,0:T(8,128)(2,1)}, bf16[768,1408]{1,0:T(8,128)(2,1)})) %all-reduce.6.cloned.1.call-update) | async-done | bytes 6488080 | tf_op jit(solution)/shard_map/psum | solution.py:86
  236.0 6.0 fusion.3
  246.7 8.4 %all-to-all-start.4 = ((bf16[32,24,512]{2,1,0:T(8,128)(2,1)}), bf16[32,24,512]{2,1,0:T(8,128)(2,1)S(1)}, u32[]{:S(2)}, u32[]{:S(2)}) async-start(bf16[32,24,512]{2,1,0:T(8,128)(2,1)} %bitcast.12), calls=%async_computation.4 | async-start | bytes 1572864 | tf_op jit(solution)/shard_map/all_to_all | solution.py:108
  255.2 4.3 fusion.21
  259.5 8.7 %all-to-all-done.4 = bf16[32,24,512]{2,1,0:T(8,128)(2,1)S(1)} async-done(((bf16[32,24,512]{2,1,0:T(8,128)(2,1)}), bf16[32,24,512]{2,1,0:T(8,128)(2,1)S(1)}, u32[]{:S(2)}, u32[]{:S(2)}) %all-to-all-start.4) | async-done | bytes 786464 | tf_op jit(solution)/shard_map/all_to_all | solution.py:108
  268.1 4.8 all-to-all-start.1
  274.6 4.3 fusion.8
  281.4 2.5 fusion.10
  283.9 2.6 gather_fusion.4
  289.5 2.6 gather_fusion.1
  293.9 3.8 multiply_reduce_fusion
  297.8 15.7 %psum.46 = f32[256,2]{0,1:T(2,128)S(1)} all-reduce(f32[256,2]{0,1:T(2,128)S(1)} %copy.60), channel_id=1, replica_groups=mesh['ctx'=32,'head'=8] {'head'}, use_global_device_ids=true, to_apply=%region_11.12 | all-reduce | flops 512 | bytes 4096 | tf_op jit(solution)/shard_map/psum | solution.py:128
  316.6 280.1 %all-reduce.4.cloned.1.call-done = f32[512,32]{0,1:T(8,128)} async-done(((f32[512,32]{0,1:T(8,128)}), f32[512,32]{0,1:T(8,128)}) %all-reduce.4.cloned.1.call-update) | async-done | bytes 65552 | tf_op jit(solution)/shard_map/psum | solution.py:139
  (87 shorter events, 29.1 us)
Async XLA Ops:
  7.2 61.2 %copy-start = (bf16[1,1408,512]{2,1,0:T(8,128)(2,1)S(1)}, bf16[1,1408,512]{2,1,0:T(8,128)(2,1)}, u32[]{:S(2)}) copy-start(bf16[1,1408,512]{2,1,0:T(8,128)(2,1)} %param.12) | copy-start | bytes 4325380
  7.2 29.4 %copy-start.1 = (bf16[256,512]{1,0:T(8,128)(2,1)S(1)}, bf16[256,512]{1,0:T(8,128)(2,1)}, u32[]{:S(2)}) copy-start(bf16[256,512]{1,0:T(8,128)(2,1)} %param.7) | copy-start | bytes 786436
  11.0 19.9 %copy-start.15 = (s32[512,1]{0,1:T(1,128)}, s32[512,1]{0,1:T(1,128)S(1)}, u32[]{:S(2)}) copy-start(s32[512,1]{0,1:T(1,128)S(1)} %compare_select_fusion) | copy-start | bytes 6148
  30.7 5.9 copy-start.7
  36.6 2.7 copy-start.2
  64.0 7.2 %copy-start.9 = (bf16[32,24,512]{2,1,0:T(8,128)(2,1)}, bf16[32,24,512]{2,1,0:T(8,128)(2,1)S(1)}, u32[]{:S(2)}) copy-start(bf16[32,24,512]{2,1,0:T(8,128)(2,1)S(1)} %all_to_all.26) | copy-start | bytes 2359300
  64.0 16.6 %all-to-all-start.3 = ((bf16[32,24,512]{2,1,0:T(8,128)(2,1)}), bf16[32,24,512]{2,1,0:T(8,128)(2,1)S(1)}, u32[]{:S(2)}, u32[]{:S(2)}) async-start(bf16[32,24,512]{2,1,0:T(8,128)(2,1)} %get-tuple-element.20), calls=%async_computation.3 | async-start | bytes 1572864 | tf_op jit(solution)/shard_map/all_to_all | solution.py:69
  68.4 167.7 %all-reduce.6.cloned.1.call-start = ((), (), s32[]{:S(2)}) async-start(), calls=%async_computation.6 | async-start | bytes 12976128 | tf_op jit(solution)/shard_map/psum | solution.py:86
  68.4 2.8 copy-start.17
  80.6 4.4 copy-start.11
  85.0 0.7 copy-start.16
  242.1 1.4 copy-start.4
  242.1 2.1 copy-start.6
  242.1 2.4 copy-start.18
  246.7 21.4 %all-to-all-start.4 = ((bf16[32,24,512]{2,1,0:T(8,128)(2,1)}), bf16[32,24,512]{2,1,0:T(8,128)(2,1)S(1)}, u32[]{:S(2)}, u32[]{:S(2)}) async-start(bf16[32,24,512]{2,1,0:T(8,128)(2,1)} %bitcast.12), calls=%async_computation.4 | async-start | bytes 1572864 | tf_op jit(solution)/shard_map/all_to_all | solution.py:108
  268.1 21.3 %all-to-all-start.1 = ((bf16[32,24,512]{2,1,0:T(8,128)(2,1)}), bf16[32,24,512]{2,1,0:T(8,128)(2,1)S(1)}, u32[]{:S(2)}, u32[]{:S(2)}) async-start(bf16[32,24,512]{2,1,0:T(8,128)(2,1)} %bitcast.81), calls=%async_computation.1 | async-start | bytes 1572864 | tf_op jit(solution)/shard_map/all_to_all | solution.py:101
  273.0 323.8 %all-reduce.4.cloned.1.call-start = ((), (), s32[]{:S(2)}) async-start(), calls=%async_computation.5 | async-start | bytes 131072 | tf_op jit(solution)/shard_map/psum | solution.py:139
  274.6 4.4 copy-start.5
  274.6 4.4 copy-start.10
  278.9 2.4 copy-start.3
  278.9 2.4 copy-start.12
  292.1 21.4 %copy-start.14 = (s32[256,2]{0,1:T(2,128)S(1)}, s32[256,2]{0,1:T(2,128)}, u32[]{:S(2)}) copy-start(s32[256,2]{0,1:T(2,128)} %param.9) | copy-start | bytes 6148
  292.1 22.3 %copy-start.8 = (bf16[256,1,512]{2,1,0:T(2,128)(2,1)S(1)}, bf16[256,1,512]{2,1,0:T(2,128)(2,1)}, u32[]{:S(2)}) copy-start(bf16[256,1,512]{2,1,0:T(2,128)(2,1)} %get-tuple-element.18) | copy-start | bytes 786436
  292.1 22.3 %copy-start.13 = (bf16[512,32]{0,1:T(8,128)(2,1)S(1)}, bf16[512,32]{0,1:T(8,128)(2,1)}, u32[]{:S(2)}) copy-start(bf16[512,32]{0,1:T(8,128)(2,1)} %param.10) | copy-start | bytes 98308
Sparse Core Ops, SparseCore 0:
  85.1 150.8 all-reduce.5
  314.5 282.1 all-reduce.3
where the time goes:
time: 606 us; the launch traced here: 605 us
  waiting for transfers between devices  433 us (71%)
  blocking collectives  64.3 us (11%)
  matrix products  31.5 us (5%)
  local copies, waits for them, and re-layouts  28.3 us (5%)
  starting transfers between devices  17.7 us (3%)
  other arithmetic  15.9 us (3%)
  between operations  14.4 us (2%)
    psum x1, waiting for transfers between devices, local(): grad_router = lax.psum(router_part, 'ctx')  280 us
    psum x1, waiting for transfers between devices, local(): lax.psum(up_part.astype(jnp.bfloat16), 'head').astype(jnp.float32)  138 us
    all_to_all x1, blocking collectives, local(): lax.all_to_all(pack_rows(tokens), 'ctx', split_axis=0, concat_axis=0, til...  20.9 us
    psum x1, blocking collectives, local(): score_grad = lax.psum(score_part, 'head')  15.7 us
    psum x1, blocking collectives, local(): lax.psum(jnp.sum(partial_logits[:, None, :] * onehot, axis=2), 'head')  15.2 us
    all_to_all x1, blocking collectives, local(): lax.all_to_all(prob_send.astype(jnp.bfloat16), 'ctx', split_axis=0, conca...  12.5 us
  transfers between devices with their start and end apart: 5, of which 4 were waited for; matrix products, arithmetic and copies ran while one was open for 5% of the time, Pallas kernels for 0%

commit v1 on v0

--- a/solution.py
+++ b/solution.py
@@ -83,7 +83,7 @@
     back_part = contract_last(cot_rows, down_w)
     gate_pre, up_pre, back_proj = (
         lax.psum(gate_part.astype(jnp.bfloat16), "head").astype(jnp.float32),
-        lax.psum(up_part.astype(jnp.bfloat16), "head").astype(jnp.float32),
+        jnp.sum(lax.all_gather(up_part.astype(jnp.bfloat16), "head"), axis=0).astype(jnp.float32),
         lax.psum(back_part.astype(jnp.bfloat16), "head").astype(jnp.float32),
     )
     hidden, gate_grad, up_grad = activations(gate_pre, up_pre, back_proj, prob_rows)

time: 606 us -> 718 us (1.18)
  waiting for transfers between devices: 433 us -> 534 us
  other arithmetic: 15.9 us -> 27.9 us
    all_gather x0 -> x1, waiting for transfers between devices: none -> 127 us  [local(): lax.all_gather(up_part.astype(jnp.bfloat16), 'head')]
    psum x1, waiting for transfers between devices: 138 us -> 110 us  [local(): lax.psum(gate_part.astype(jnp.bfloat16), 'head').astype(jnp.float32)]
    reduce_sum x0 -> x1, other arithmetic: none -> 10.7 us  [local(): jnp.sum(lax.all_gather(up_part.astype(jnp.bfloat16), 'head'), axis=0)]
    all_to_all x1, waiting for transfers between devices: 8.67 us -> 0.01 us  [local(): lax.all_to_all(dx_rows.reshape(ctx_count, capacity, shard_width), 'ctx',...]
  transfers between devices with their start and end apart: 5 -> 6, of which waited for: 4 -> 5; matrix products, arithmetic and copies ran while one was open for 5% -> 6% of each run, Pallas kernels for 0% -> 0%
where the time goes in v1:
time: 718 us; the launch traced here: 717 us
  waiting for transfers between devices  534 us (74%)
  blocking collectives  63.8 us (9%)
  matrix products  30.1 us (4%)
  local copies, waits for them, and re-layouts  29.9 us (4%)
  other arithmetic  27.9 us (4%)
  starting transfers between devices  16.7 us (2%)
  between operations  14.1 us (2%)
    psum x1, waiting for transfers between devices, local(): grad_router = lax.psum(router_part, 'ctx')  283 us
    all_gather x1, waiting for transfers between devices, local(): lax.all_gather(up_part.astype(jnp.bfloat16), 'head')  127 us
    psum x1, waiting for transfers between devices, local(): lax.psum(gate_part.astype(jnp.bfloat16), 'head').astype(jnp.float32)  110 us
    all_to_all x1, blocking collectives, local(): lax.all_to_all(pack_rows(tokens), 'ctx', split_axis=0, concat_axis=0, til...  20.9 us
    psum x1, blocking collectives, local(): lax.psum(jnp.sum(partial_logits[:, None, :] * onehot, axis=2), 'head')  15.8 us
  transfers between devices with their start and end apart: 6, of which 5 were waited for; matrix products, arithmetic and copies ran while one was open for 6% of the time, Pallas kernels for 0%

profile of v1, /device:TPU:64, one launch (start us, length us, event | category | flops | bytes accessed | tf_op | source)
XLA Modules:
  0.0 717.0 jit_solution(14111129826106009604)
XLA Ops:
  13.6 2.7 gather_fusion.3
  16.3 2.7 gather_fusion
  19.9 15.8 %psum.35 = f32[256,2]{0,1:T(2,128)} all-reduce(f32[256,2]{0,1:T(2,128)S(1)} %select_reduce_fusion.1), channel_id=1, replica_groups=mesh['ctx'=32,'head'=8] {'head'}, use_global_device_ids=true, to_apply=%region_1.0 | all-reduce | flops 512 | bytes 4096 | tf_op jit(solution)/shard_map/psum | solution.py:42
  40.2 6.7 gather_fusion.2
  50.0 20.9 %all_to_all.26 = bf16[32,24,512]{2,1,0:T(8,128)(2,1)S(1)} all-to-all(bf16[32,24,512]{2,1,0:T(8,128)(2,1)S(1)} %get-tuple-element.20), channel_id=1, replica_groups=mesh['ctx'=32,'head'=8] {'ctx'}, dimensions={0} | all-to-all | bytes 1572864 | tf_op jit(solution)/shard_map/all_to_all | solution.py:68
  70.9 2.8 convolution_convert_fusion.1
  73.7 4.4 all-to-all-start.3
  78.2 4.2 convolution_convert_fusion.2
  82.4 8.0 %all-to-all-done.3 = bf16[32,24,512]{2,1,0:T(8,128)(2,1)S(1)} async-done(((bf16[32,24,512]{2,1,0:T(8,128)(2,1)}), bf16[32,24,512]{2,1,0:T(8,128)(2,1)S(1)}, u32[]{:S(2)}, u32[]{:S(2)}) %all-to-all-start.3) | async-done | bytes 786464 | tf_op jit(solution)/shard_map/all_to_all | solution.py:69
  90.3 2.8 convolution_convert_fusion
  93.2 13.2 %all_to_all.27 = bf16[32,1,24]{2,1,0:T(2,128)(2,1)S(1)} all-to-all(bf16[32,1,24]{2,1,0:T(2,128)(2,1)S(1)} %convert_element_type.139), channel_id=1, replica_groups=mesh['ctx'=32,'head'=8] {'ctx'}, dimensions={0} | all-to-all | bytes 3072 | tf_op jit(solution)/shard_map/all_to_all | solution.py:70
  106.6 127.2 %all-gather.3.cloned.1.call-done = bf16[6144,1408]{1,0:T(8,128)(2,1)} async-done(((bf16[768,1408]{1,0:T(8,128)(2,1)}), bf16[6144,1408]{1,0:T(8,128)(2,1)}) %all-gather.3.cloned.1.call-update) | async-done | bytes 17301520 | tf_op jit(solution)/shard_map/all_gather | solution.py:86
  233.8 10.7 %reduce_sum.62 = bf16[768,1408]{1,0:T(8,128)(2,1)} reduce(bf16[8,768,1408]{2,1,0:T(8,128)(2,1)} %bitcast.74, bf16[]{:T(256)} %constant.45.clone.1), dimensions={0}, to_apply=%region_7.8 | reduce | flops 7569408 | bytes 19464194 | tf_op jit(solution)/shard_map/reduce_sum | solution.py:86
  244.5 109.7 %all-reduce.6.cloned.1.call-done = (bf16[768,1408]{1,0:T(8,128)(2,1)}, bf16[768,1408]{1,0:T(8,128)(2,1)}) async-done(((bf16[768,1408]{1,0:T(8,128)(2,1)}, bf16[768,1408]{1,0:T(8,128)(2,1)}), (bf16[768,1408]{1,0:T(8,128)(2,1)}, bf16[768,1408]{1,0:T(8,128)(2,1)})) %all-reduce.6.cloned.1.call-update) | async-done | bytes 4325392 | tf_op jit(solution)/shard_map/psum | solution.py:85
  354.2 6.4 fusion.3
  362.9 7.5 %all-to-all-start.1 = ((bf16[32,24,512]{2,1,0:T(8,128)(2,1)}), bf16[32,24,512]{2,1,0:T(8,128)(2,1)S(1)}, u32[]{:S(2)}, u32[]{:S(2)}) async-start(bf16[32,24,512]{2,1,0:T(8,128)(2,1)} %bitcast.9), calls=%async_computation.1 | async-start | bytes 1572864 | tf_op jit(solution)/shard_map/all_to_all | solution.py:101
  371.3 3.5 fusion.15
  377.1 6.4 all-to-all-done.1
  383.5 4.7 all-to-all-start.4
  388.3 4.4 fusion.8
  400.2 2.7 reshape.149
  402.9 4.0 multiply_reduce_fusion
  407.0 13.9 %psum.38 = f32[256,2]{0,1:T(2,128)S(1)} all-reduce(f32[256,2]{0,1:T(2,128)S(1)} %copy.60), channel_id=1, replica_groups=mesh['ctx'=32,'head'=8] {'head'}, use_global_device_ids=true, to_apply=%region_11.12 | all-reduce | flops 512 | bytes 4096 | tf_op jit(solution)/shard_map/psum | solution.py:128
  425.9 283.0 %all-reduce.4.cloned.1.call-done = f32[512,32]{0,1:T(8,128)} async-done(((f32[512,32]{0,1:T(8,128)}), f32[512,32]{0,1:T(8,128)}) %all-reduce.4.cloned.1.call-update) | async-done | bytes 65552 | tf_op jit(solution)/shard_map/psum | solution.py:139
  (97 shorter events, 34.6 us)
Async XLA Ops:
  7.2 83.2 %copy-start = (bf16[1,1408,512]{2,1,0:T(8,128)(2,1)S(1)}, bf16[1,1408,512]{2,1,0:T(8,128)(2,1)}, u32[]{:S(2)}) copy-start(bf16[1,1408,512]{2,1,0:T(8,128)(2,1)} %param.13) | copy-start | bytes 4325380
  7.2 6.4 copy-start.2
  7.2 226.6 %all-gather.3.cloned.1.call-start = ((), (), s32[]{:S(2)}) async-start(), calls=%async_computation.6 | async-start | bytes 19464192 | tf_op jit(solution)/shard_map/all_gather | solution.py:86
  11.0 2.5 copy-start.18
  13.5 2.7 copy-start.1
  16.3 3.6 copy-start.13
  48.9 22.0 %copy-start.20 = (bf16[1,1408,512]{2,1,0:T(8,128)(2,1)S(1)}, bf16[1,1408,512]{2,1,0:T(8,128)(2,1)}, u32[]{:S(2)}) copy-start(bf16[1,1408,512]{2,1,0:T(8,128)(2,1)} %param.12) | copy-start | bytes 4325380
  70.9 7.3 %copy-start.8 = (bf16[32,24,512]{2,1,0:T(8,128)(2,1)}, bf16[32,24,512]{2,1,0:T(8,128)(2,1)S(1)}, u32[]{:S(2)}) copy-start(bf16[32,24,512]{2,1,0:T(8,128)(2,1)S(1)} %all_to_all.26) | copy-start | bytes 2359300
  73.7 16.6 %all-to-all-start.3 = ((bf16[32,24,512]{2,1,0:T(8,128)(2,1)}), bf16[32,24,512]{2,1,0:T(8,128)(2,1)S(1)}, u32[]{:S(2)}, u32[]{:S(2)}) async-start(bf16[32,24,512]{2,1,0:T(8,128)(2,1)} %get-tuple-element.19), calls=%async_computation.3 | async-start | bytes 1572864 | tf_op jit(solution)/shard_map/all_to_all | solution.py:69
  78.1 276.1 %all-reduce.6.cloned.1.call-start = ((), (), s32[]{:S(2)}) async-start(), calls=%async_computation.7 | async-start | bytes 8650752 | tf_op jit(solution)/shard_map/psum | solution.py:85
  90.3 2.8 copy-start.10
  362.9 8.3 %copy-start.19 = (s32[512,1]{0,1:T(1,128)S(1)}, s32[512,1]{0,1:T(1,128)}, u32[]{:S(2)}) copy-start(s32[512,1]{0,1:T(1,128)} %copy-done.18) | copy-start | bytes 6148
  362.9 20.6 %all-to-all-start.1 = ((bf16[32,24,512]{2,1,0:T(8,128)(2,1)}), bf16[32,24,512]{2,1,0:T(8,128)(2,1)S(1)}, u32[]{:S(2)}, u32[]{:S(2)}) async-start(bf16[32,24,512]{2,1,0:T(8,128)(2,1)} %bitcast.9), calls=%async_computation.1 | async-start | bytes 1572864 | tf_op jit(solution)/shard_map/all_to_all | solution.py:101
  371.3 3.6 copy-start.6
  371.3 3.6 copy-start.21
  383.5 37.4 %all-to-all-start.4 = ((bf16[32,24,512]{2,1,0:T(8,128)(2,1)}), bf16[32,24,512]{2,1,0:T(8,128)(2,1)S(1)}, u32[]{:S(2)}, u32[]{:S(2)}) async-start(bf16[32,24,512]{2,1,0:T(8,128)(2,1)} %bitcast.83), calls=%async_computation.4 | async-start | bytes 1572864 | tf_op jit(solution)/shard_map/all_to_all | solution.py:108
  388.2 320.8 %all-reduce.4.cloned.1.call-start = ((), (), s32[]{:S(2)}) async-start(), calls=%async_computation.5 | async-start | bytes 131072 | tf_op jit(solution)/shard_map/psum | solution.py:139
  388.2 4.4 copy-start.5
  388.2 4.4 copy-start.9
  392.6 2.5 copy-start.4
  392.6 2.4 copy-start.11
  397.6 5.3 copy-start.7
  400.2 20.6 %copy-start.15 = (f32[256,1]{0,1:T(1,128)S(1)}, f32[256,1]{0,1:T(1,128)}, u32[]{:S(2)}) copy-start(f32[256,1]{0,1:T(1,128)} %copy-done.14) | copy-start | bytes 3076
  400.2 20.6 %copy-start.17 = (f32[256,1]{0,1:T(1,128)S(1)}, f32[256,1]{0,1:T(1,128)}, u32[]{:S(2)}) copy-start(f32[256,1]{0,1:T(1,128)} %copy-done.16) | copy-start | bytes 3076
  (4 other events, 5.8 us)
Sparse Core Ops, SparseCore 0:
  73.9 159.9 all-gather.2
  236.5 117.6 all-reduce.5
  424.9 284.0 all-reduce.3
